TPU v7x, 32 devices: a whole 2x2x4 slice. The times are simulated.
32 devices in a mesh: row: 8 (over y, x, core), col: 4 (over z).
Axes of the slice: x: 2, y: 2, z: 4, core: 2. Of those that a mesh axis runs over, the one named last changes fastest.
Arguments:
- pair_rep: bfloat16 [128, 128, 128], P(('row', 'col')), may hold values from -16 to 16
- tile_mask: int32 [1, 1], replicated, may hold values from 0 to 1, as said below
- chain_ids: int32 [128], replicated, may hold values from 0 to 3, never falling along the last dimension, each value on 1 to 64 neighbouring positions
- chain_bias: float32 [2, 4], replicated, may hold values from -6 to 6
- row_project: bfloat16 [128, 512], replicated, may hold values from -0.5 to 0.5
- row_bias_proj: bfloat16 [128, 4], replicated, may hold values from -36 to 36
- row_output: bfloat16 [128, 128], replicated, may hold values from -0.5 to 0.5
- col_project: bfloat16 [128, 512], replicated, may hold values from -0.5 to 0.5
- col_bias_proj: bfloat16 [128, 4], replicated, may hold values from -36 to 36
- col_output: bfloat16 [128, 128], replicated, may hold values from -0.5 to 0.5
- tri_left: bfloat16 [128, 256], replicated, may hold values from -0.5 to 0.5
- tri_right: bfloat16 [128, 256], replicated, may hold values from -0.5 to 0.5
- tri_gate: bfloat16 [128, 128], replicated, may hold values from -0.5 to 0.5
- tri_output: bfloat16 [128, 128], replicated, may hold values from -1.5 to 1.5
Outputs:
- pair_out: bfloat16 [128, 128, 128], P('row', 'col')
Inputs may be any that keep to these rules, and one draw needn't show every extreme that they name: `tile_mask`: every diagonal entry is 1. `chain_ids`: chain numbers never fall along the residues.
All inputs are finite; a program needn't handle non-finite values.
Results may differ from a plain program's by a relative error of at most 0.018.
Values may be sent and summed in bfloat16 or wider, within the bound.
No kernel may reach another device: no remote copies, remote signals or barrier semaphores. Data moves between devices by JAX's collectives and lax.ppermute only.
A program may use at most 64 MiB of HBM per device.

v0:
```python
import jax
import jax.numpy as jnp
from jax import lax
from jax.sharding import PartitionSpec as P


def layer_norm(values):
    values = values.astype(jnp.float32)
    center = values - jnp.mean(values, axis=-1, keepdims=True)
    spread = jnp.mean(center * center, axis=-1, keepdims=True)
    return center * lax.rsqrt(spread + 1e-05)


def tile_rows(positions, tile_table, length):
    tile_count = tile_table.shape[0]
    tile_width = length // tile_count
    onehot = (positions[:, None] // tile_width == jnp.arange(tile_count)[None, :]).astype(
        jnp.float32
    )
    picked = jnp.dot(onehot, tile_table.astype(jnp.float32))
    spread_out = jnp.broadcast_to(picked[:, :, None], (positions.shape[0], tile_count, tile_width))
    return spread_out.reshape(positions.shape[0], length) > 0.5


def tile_pairs(row_pos, col_pos, tile_table, length):
    tile_count = tile_table.shape[0]
    tile_width = length // tile_count
    row_hot = (row_pos[:, None] // tile_width == jnp.arange(tile_count)[None, :]).astype(
        jnp.float32
    )
    col_hot = (col_pos[:, None] // tile_width == jnp.arange(tile_count)[None, :]).astype(
        jnp.float32
    )
    return jnp.dot(jnp.dot(row_hot, tile_table.astype(jnp.float32)), col_hot.T)


def attend_lines(
    queries,
    key_rows,
    value_rows,
    gate_pre,
    bias_all,
    key_ok,
    chain_ids,
    chain_add,
    line_dim,
    flipped,
):
    line_count = queries.shape[line_dim]
    length = queries.shape[1 - line_dim]
    head_count = queries.shape[2]
    head_size = queries.shape[3]
    width_all = head_count * head_size
    query_rows = min(128, length)
    per_line = length // query_rows
    scaling = head_size ** (-0.5)

    def one_block(block_index):
        line_index = block_index // per_line
        offset = block_index % per_line * query_rows
        query_line = lax.dynamic_index_in_dim(queries, line_index, line_dim, keepdims=False)
        query_block = lax.dynamic_slice_in_dim(query_line, offset, query_rows, 0)
        key_line = lax.dynamic_index_in_dim(key_rows, line_index, line_dim, keepdims=False)
        value_line = lax.dynamic_index_in_dim(value_rows, line_index, line_dim, keepdims=False)
        scores = (
            jnp.einsum("qhd,khd->hqk", query_block, key_line, preferred_element_type=jnp.float32)
            * scaling
        )
        if flipped:
            bias_block = lax.dynamic_slice_in_dim(bias_all, offset, query_rows, 2).transpose(
                0, 2, 1
            )
        else:
            bias_block = lax.dynamic_slice_in_dim(bias_all, offset, query_rows, 1)
        scores = scores + bias_block
        chain_block = lax.dynamic_slice_in_dim(chain_ids, offset, query_rows, 0)
        same_chain = (chain_block[:, None] == chain_ids[None, :]).astype(jnp.float32)
        scores = scores + chain_add[:, None, None] * same_chain[None]
        usable = lax.dynamic_index_in_dim(key_ok, line_index, 0, keepdims=False)
        scores = jnp.where(usable[None, None, :], scores, -1000000000.0)
        row_peak = jnp.max(scores, axis=-1, keepdims=True)
        weights = jnp.exp(scores - row_peak)
        attention = (weights / jnp.sum(weights, axis=-1, keepdims=True)).astype(jnp.bfloat16)
        mixed_rows = jnp.einsum(
            "hqk,khd->qhd", attention, value_line, preferred_element_type=jnp.float32
        ).reshape(query_rows, width_all)
        gate_line = lax.dynamic_index_in_dim(gate_pre, line_index, line_dim, keepdims=False)
        gate_block = lax.dynamic_slice_in_dim(gate_line, offset, query_rows, 0)
        return (mixed_rows * jax.nn.sigmoid(gate_block)).astype(jnp.bfloat16)

    outputs = lax.map(one_block, jnp.arange(line_count * per_line, dtype=jnp.int32))
    outputs = outputs.reshape(line_count, length, width_all)
    if line_dim == 1:
        outputs = outputs.transpose(1, 0, 2)
    return outputs


def tri_acts(normed, weights, allowed):
    channels = normed.shape[-1]
    projected = jnp.dot(normed.reshape(-1, channels), weights, preferred_element_type=jnp.float32)
    projected = projected.reshape(normed.shape[0], normed.shape[1], 2 * channels)
    return (
        jax.nn.sigmoid(projected[..., channels:]) * projected[..., :channels] * allowed[..., None]
    ).astype(jnp.bfloat16)


def shards(
    pair_rep,
    tile_mask,
    chain_ids,
    chain_bias,
    row_project,
    row_bias_proj,
    row_output,
    col_project,
    col_bias_proj,
    col_output,
    tri_left,
    tri_right,
    tri_gate,
    tri_output,
):
    n_row = lax.axis_size("row")
    n_col = lax.axis_size("col")
    device_count = n_row * n_col
    rows_here, length, channels = pair_rep.shape
    head_count = row_bias_proj.shape[1]
    head_size = channels // head_count
    row_index = lax.axis_index("row")
    col_index = lax.axis_index("col")
    device_index = row_index * n_col + col_index
    local_lines = device_index * rows_here + jnp.arange(rows_here, dtype=jnp.int32)
    normed = layer_norm(pair_rep).astype(jnp.bfloat16)
    flat_rows = normed.reshape(rows_here * length, channels)
    bias_rows = jnp.dot(flat_rows, row_bias_proj, preferred_element_type=jnp.float32)
    bias_rows = bias_rows.reshape(rows_here, length, head_count).transpose(2, 0, 1)
    bias_all = lax.all_gather(bias_rows, ("row", "col"), axis=1, tiled=True)
    projected = jnp.dot(flat_rows, row_project, preferred_element_type=jnp.float32).reshape(
        rows_here, length, 4 * channels
    )
    qkv_rows = (
        projected[..., : 3 * channels]
        .astype(jnp.bfloat16)
        .reshape(rows_here, length, 3, head_count, head_size)
    )
    key_ok = tile_rows(local_lines, tile_mask, length)
    mixed_rows = attend_lines(
        qkv_rows[:, :, 0],
        qkv_rows[:, :, 1],
        qkv_rows[:, :, 2],
        projected[..., 3 * channels :],
        bias_all,
        key_ok,
        chain_ids,
        chain_bias[0],
        0,
        False,
    )
    update = jnp.dot(
        mixed_rows.reshape(-1, channels), row_output, preferred_element_type=jnp.float32
    ).reshape(rows_here, length, channels)
    first_pair = (pair_rep.astype(jnp.float32) + update).astype(jnp.bfloat16)
    normed_first = layer_norm(first_pair).astype(jnp.bfloat16)
    bias_next = jnp.dot(
        normed_first.reshape(-1, channels), col_bias_proj, preferred_element_type=jnp.float32
    )
    bias_next = bias_next.reshape(rows_here, length, head_count).transpose(2, 0, 1)
    bias_cols = lax.all_gather(bias_next, ("row", "col"), axis=1, tiled=True)
    columns = lax.all_to_all(first_pair, ("row", "col"), split_axis=1, concat_axis=0, tiled=True)
    normed_cols = layer_norm(columns).astype(jnp.bfloat16)
    projected_cols = jnp.dot(
        normed_cols.reshape(-1, channels), col_project, preferred_element_type=jnp.float32
    ).reshape(length, rows_here, 4 * channels)
    qkv_cols = (
        projected_cols[..., : 3 * channels]
        .astype(jnp.bfloat16)
        .reshape(length, rows_here, 3, head_count, head_size)
    )
    col_ok = tile_rows(local_lines, tile_mask.T, length)
    mixed_cols = attend_lines(
        qkv_cols[:, :, 0],
        qkv_cols[:, :, 1],
        qkv_cols[:, :, 2],
        projected_cols[..., 3 * channels :],
        bias_cols,
        col_ok,
        chain_ids,
        chain_bias[1],
        1,
        True,
    )
    update_cols = jnp.dot(
        mixed_cols.reshape(-1, channels), col_output, preferred_element_type=jnp.float32
    ).reshape(length, rows_here, channels)
    second_pair = (columns.astype(jnp.float32) + update_cols).astype(jnp.bfloat16)
    normed_second = layer_norm(second_pair).astype(jnp.bfloat16)
    edge_mask = tile_pairs(jnp.arange(length, dtype=jnp.int32), local_lines, tile_mask, length)
    left_all = tri_acts(normed_second, tri_left, edge_mask)
    right_all = tri_acts(normed_second, tri_right, edge_mask)
    block_rows = length // n_row
    block_cols = length // n_col

    def one_round(round_index, loop_state):
        product_sum, own_block = loop_state
        left_col = lax.dynamic_index_in_dim(left_all, round_index, 1, keepdims=False)
        right_col = lax.dynamic_index_in_dim(right_all, round_index, 1, keepdims=False)
        raw_col = lax.dynamic_index_in_dim(second_pair, round_index, 1, keepdims=False)
        left_send = jnp.broadcast_to(
            left_col.reshape(n_row, 1, block_rows, channels), (n_row, n_col, block_rows, channels)
        )
        raw_send = jnp.broadcast_to(
            raw_col.reshape(n_row, 1, block_rows, channels), (n_row, n_col, block_rows, channels)
        )
        right_send = jnp.broadcast_to(
            right_col.reshape(1, n_col, block_cols, channels), (n_row, n_col, block_cols, channels)
        )
        outgoing = jnp.concatenate([left_send, raw_send, right_send], axis=2).reshape(
            device_count, 2 * block_rows + block_cols, channels
        )
        received = lax.all_to_all(outgoing, ("row", "col"), split_axis=0, concat_axis=0, tiled=True)
        left_act = received[:, :block_rows].transpose(1, 0, 2)
        right_act = received[:, 2 * block_rows :].transpose(1, 0, 2)
        product_sum = product_sum + jnp.einsum(
            "ikc,jkc->ijc", left_act, right_act, preferred_element_type=jnp.float32
        )
        own_piece = lax.dynamic_slice_in_dim(
            received[:, block_rows : 2 * block_rows], col_index * n_row, n_row, 0
        )
        own_block = lax.dynamic_update_index_in_dim(own_block, own_piece, round_index, 1)
        return (product_sum, own_block)

    initial = (
        jnp.zeros((block_rows, block_cols, channels), jnp.float32),
        jnp.zeros((n_row, rows_here, block_rows, channels), jnp.bfloat16),
    )
    product_sum, own_block = lax.fori_loop(0, rows_here, one_round, initial)
    own_pair = own_block.transpose(2, 0, 1, 3).reshape(block_rows, block_cols, channels)
    normed_own = layer_norm(own_pair).astype(jnp.bfloat16)
    gate_values = jax.nn.sigmoid(
        jnp.dot(normed_own.reshape(-1, channels), tri_gate, preferred_element_type=jnp.float32)
    ).reshape(block_rows, block_cols, channels)
    centered = layer_norm(product_sum).astype(jnp.bfloat16)
    update_tri = jnp.dot(
        centered.reshape(-1, channels), tri_output, preferred_element_type=jnp.float32
    ).reshape(block_rows, block_cols, channels)
    return (own_pair.astype(jnp.float32) + gate_values * update_tri).astype(jnp.bfloat16)


def solution(mesh):
    return jax.shard_map(
        shards,
        mesh=mesh,
        in_specs=(
            P(("row", "col"), None, None),
            P(),
            P(),
            P(),
            P(),
            P(),
            P(),
            P(),
            P(),
            P(),
            P(),
            P(),
            P(),
            P(),
        ),
        out_specs=P("row", "col", None),
        check_vma=False,
    )
```

profile of v0, /device:TPU:1, one launch (start us, length us, event | category | flops | bytes accessed | tf_op | source)
XLA Modules:
  0.0 284.5 jit_solution(12374093587075202309)
XLA Ops:
  0.0 1.1 copy.107
  1.6 0.9 copy-done.1
  4.7 66.4 %all_gather.6 = f32[4,128,128]{2,0,1:T(4,128)S(1)} all-gather(f32[4,4,128]{2,0,1:T(4,128)S(1)} %convolution_bitcast_fusion.2), channel_id=1, replica_groups=mesh['row'=8,'col'=4] {'row','col'}, dimensions={1}, use_global_device_ids=true | all-gather | bytes 270336 | tf_op jit(solution)/shard_map/all_gather | solution.py:137
  72.5 14.2 %while.42 = (s32[]{:T(128)}, bf16[4,128,128]{1,2,0:T(8,128)(2,1)S(1)}, s32[4]{0:T(128)S(1)}, bf16[4,128,4,32]{1,3,2,0:T(8,128)(2,1)S(1)}, pred[4,128]{1,0:T(4,12...) while((s32[]{:T(128)}, ...), condition=%wide.region_5.6_spmd, body=%wide.region_2.5_spmd.sunk | while | flops 9159427 | bytes 2038731 | solution.py:91
  88.6 65.4 %all_gather.7 = f32[4,128,128]{2,0,1:T(4,128)S(1)} all-gather(f32[4,4,128]{2,0,1:T(4,128)S(1)} %convolution_bitcast_fusion.1), channel_id=1, replica_groups=mesh['row'=8,'col'=4] {'row','col'}, dimensions={1}, use_global_device_ids=true | all-gather | bytes 270336 | tf_op jit(solution)/shard_map/all_gather | solution.py:168
  154.1 7.7 %all-to-all-start.1 = ((bf16[4,128,128]{2,0,1:T(4,128)(2,1)}), bf16[4,128,128]{2,0,1:T(4,128)(2,1)S(1)}, u32[]{:S(2)}, u32[]{:S(2)}) async-start(bf16[4,128,128]{2,0,1:T(4,128)(2,1)} %copy.115), calls=%async_computation.1 | async-start | bytes 262144 | tf_op jit(solution)/shard_map/all_to_all | solution.py:169
  161.9 7.3 %all-to-all-done.1 = bf16[4,128,128]{2,0,1:T(4,128)(2,1)S(1)} async-done(((bf16[4,128,128]{2,0,1:T(4,128)(2,1)}), bf16[4,128,128]{2,0,1:T(4,128)(2,1)S(1)}, u32[]{:S(2)}, u32[]{:S(2)}) %all-to-all-start.1) | async-done | bytes 131104 | tf_op jit(solution)/shard_map/all_to_all | solution.py:169
  172.6 13.4 %while.43 = (s32[]{:T(128)}, bf16[4,128,128]{1,2,0:T(8,128)(2,1)S(1)}, s32[4]{0:T(128)S(1)}, bf16[128,4,4,32]{0,3,2,1:T(8,128)(2,1)S(1)}, pred[4,128]{1,0:T(4,12...) while((s32[]{:T(128)}, ...), condition=%wide.region_13.14_spmd, body=%wide.region_10.13_spmd.sunk | while | flops 9159427 | bytes 2038731 | solution.py:91
  188.4 92.2 %while.44 = (s32[]{:T(128)}, f32[16,32,128]{1,0,2:T(8,128)S(1)}, bf16[8,4,16,128]{3,2,0,1:T(8,128)(2,1)S(1)}, bf16[128,4,128]{2,0,1:T(8,128)(2,1)S(1)}, bf16[128...) while((s32[]{:T(128)}, f32[16,32,128]{1,0,2:T(8,128)S(1)}, ...), condition=%wide.region_17.18_spmd.clone, body=%wide.region_16.17_spmd.clone.sunk | while | flops 5898243 | bytes 7373015 | solution.py:236
  189.2 0.9 pad_maximum_fusion.2
  190.0 3.5 %all-to-all-start = ((bf16[32,64,128]{2,1,0:T(8,128)(2,1)}), bf16[32,64,128]{2,1,0:T(8,128)(2,1)S(1)}, u32[]{:S(2)}, u32[]{:S(2)}) async-start(bf16[32,64,128]{2,1,0:T(8,128)(2,1)} %bitcast.188), calls=%async_computation | async-start | bytes 1048576 | tf_op jit(solution)/shard_map/while/body/eval_jaxpr/all_to_all | solution.py:220
  193.5 15.4 %all-to-all-done = bf16[32,64,128]{2,1,0:T(8,128)(2,1)S(1)} async-done(((bf16[32,64,128]{2,1,0:T(8,128)(2,1)}), bf16[32,64,128]{2,1,0:T(8,128)(2,1)S(1)}, u32[]{:S(2)}, u32[]{:S(2)}) %all-to-all-start) | async-done | bytes 524320 | tf_op jit(solution)/shard_map/while/body/eval_jaxpr/all_to_all | solution.py:220
  209.4 1.4 copy.177
  212.6 0.9 pad_maximum_fusion.2
  213.4 3.1 %all-to-all-start = ((bf16[32,64,128]{2,1,0:T(8,128)(2,1)}), bf16[32,64,128]{2,1,0:T(8,128)(2,1)S(1)}, u32[]{:S(2)}, u32[]{:S(2)}) async-start(bf16[32,64,128]{2,1,0:T(8,128)(2,1)} %bitcast.188), calls=%async_computation | async-start | bytes 1048576 | tf_op jit(solution)/shard_map/while/body/eval_jaxpr/all_to_all | solution.py:220
  216.6 15.3 %all-to-all-done = bf16[32,64,128]{2,1,0:T(8,128)(2,1)S(1)} async-done(((bf16[32,64,128]{2,1,0:T(8,128)(2,1)}), bf16[32,64,128]{2,1,0:T(8,128)(2,1)S(1)}, u32[]{:S(2)}, u32[]{:S(2)}) %all-to-all-start) | async-done | bytes 524320 | tf_op jit(solution)/shard_map/while/body/eval_jaxpr/all_to_all | solution.py:220
  232.3 1.4 copy.177
  236.3 3.2 %all-to-all-start = ((bf16[32,64,128]{2,1,0:T(8,128)(2,1)}), bf16[32,64,128]{2,1,0:T(8,128)(2,1)S(1)}, u32[]{:S(2)}, u32[]{:S(2)}) async-start(bf16[32,64,128]{2,1,0:T(8,128)(2,1)} %bitcast.188), calls=%async_computation | async-start | bytes 1048576 | tf_op jit(solution)/shard_map/while/body/eval_jaxpr/all_to_all | solution.py:220
  239.5 15.3 %all-to-all-done = bf16[32,64,128]{2,1,0:T(8,128)(2,1)S(1)} async-done(((bf16[32,64,128]{2,1,0:T(8,128)(2,1)}), bf16[32,64,128]{2,1,0:T(8,128)(2,1)S(1)}, u32[]{:S(2)}, u32[]{:S(2)}) %all-to-all-start) | async-done | bytes 524320 | tf_op jit(solution)/shard_map/while/body/eval_jaxpr/all_to_all | solution.py:220
  255.3 1.4 copy.177
  259.3 3.2 %all-to-all-start = ((bf16[32,64,128]{2,1,0:T(8,128)(2,1)}), bf16[32,64,128]{2,1,0:T(8,128)(2,1)S(1)}, u32[]{:S(2)}, u32[]{:S(2)}) async-start(bf16[32,64,128]{2,1,0:T(8,128)(2,1)} %bitcast.188), calls=%async_computation | async-start | bytes 1048576 | tf_op jit(solution)/shard_map/while/body/eval_jaxpr/all_to_all | solution.py:220
  262.4 15.3 %all-to-all-done = bf16[32,64,128]{2,1,0:T(8,128)(2,1)S(1)} async-done(((bf16[32,64,128]{2,1,0:T(8,128)(2,1)}), bf16[32,64,128]{2,1,0:T(8,128)(2,1)S(1)}, u32[]{:S(2)}, u32[]{:S(2)}) %all-to-all-start) | async-done | bytes 524320 | tf_op jit(solution)/shard_map/while/body/eval_jaxpr/all_to_all | solution.py:220
  278.2 1.4 copy.177
  283.6 1.0 fusion.41
  (230 shorter events, 35.1 us)
Async XLA Ops:
  0.0 1.2 copy-start
  1.5 1.0 copy-start.1
  3.2 0.7 copy-start.11
  3.9 0.7 copy-start.13
  71.5 1.0 slice-start
  71.6 0.8 copy-start.4
  72.5 14.2 %copy-start.10 = (bf16[128,128]{1,0:T(8,128)(2,1)S(1)}, bf16[128,128]{1,0:T(8,128)(2,1)}, u32[]{:S(2)}) copy-start(bf16[128,128]{1,0:T(8,128)(2,1)} %param.26) | copy-start | bytes 98308
  87.8 0.7 copy-start.14
  154.1 15.1 %all-to-all-start.1 = ((bf16[4,128,128]{2,0,1:T(4,128)(2,1)}), bf16[4,128,128]{2,0,1:T(4,128)(2,1)S(1)}, u32[]{:S(2)}, u32[]{:S(2)}) async-start(bf16[4,128,128]{2,0,1:T(4,128)(2,1)} %copy.115), calls=%async_computation.1 | async-start | bytes 262144 | tf_op jit(solution)/shard_map/all_to_all | solution.py:169
  170.9 0.9 copy-start.5
  172.6 13.4 %copy-start.8 = (bf16[128,128]{1,0:T(8,128)(2,1)S(1)}, bf16[128,128]{1,0:T(8,128)(2,1)}, u32[]{:S(2)}) copy-start(bf16[128,128]{1,0:T(8,128)(2,1)} %param.29) | copy-start | bytes 98308
  186.3 0.8 copy-start.6
  187.1 0.8 copy-start.7
  188.4 0.7 copy-start.2
  190.0 18.9 %all-to-all-start = ((bf16[32,64,128]{2,1,0:T(8,128)(2,1)}), bf16[32,64,128]{2,1,0:T(8,128)(2,1)S(1)}, u32[]{:S(2)}, u32[]{:S(2)}) async-start(bf16[32,64,128]{2,1,0:T(8,128)(2,1)} %bitcast.188), calls=%async_computation | async-start | bytes 1048576 | tf_op jit(solution)/shard_map/while/body/eval_jaxpr/all_to_all | solution.py:220
  210.9 0.9 copy-start.3
  213.4 18.4 %all-to-all-start = ((bf16[32,64,128]{2,1,0:T(8,128)(2,1)}), bf16[32,64,128]{2,1,0:T(8,128)(2,1)S(1)}, u32[]{:S(2)}, u32[]{:S(2)}) async-start(bf16[32,64,128]{2,1,0:T(8,128)(2,1)} %bitcast.188), calls=%async_computation | async-start | bytes 1048576 | tf_op jit(solution)/shard_map/while/body/eval_jaxpr/all_to_all | solution.py:220
  233.8 0.9 copy-start.3
  236.3 18.4 %all-to-all-start = ((bf16[32,64,128]{2,1,0:T(8,128)(2,1)}), bf16[32,64,128]{2,1,0:T(8,128)(2,1)S(1)}, u32[]{:S(2)}, u32[]{:S(2)}) async-start(bf16[32,64,128]{2,1,0:T(8,128)(2,1)} %bitcast.188), calls=%async_computation | async-start | bytes 1048576 | tf_op jit(solution)/shard_map/while/body/eval_jaxpr/all_to_all | solution.py:220
  256.8 0.9 copy-start.3
  259.3 18.4 %all-to-all-start = ((bf16[32,64,128]{2,1,0:T(8,128)(2,1)}), bf16[32,64,128]{2,1,0:T(8,128)(2,1)S(1)}, u32[]{:S(2)}, u32[]{:S(2)}) async-start(bf16[32,64,128]{2,1,0:T(8,128)(2,1)} %bitcast.188), calls=%async_computation | async-start | bytes 1048576 | tf_op jit(solution)/shard_map/while/body/eval_jaxpr/all_to_all | solution.py:220
  279.7 0.9 copy-start.3
  282.0 0.8 copy-start.12
  282.8 0.8 copy-start.9
  (3 other events, 2.0 us)
where the time goes:
time: 286 us; the launch traced here: 285 us
  blocking collectives  132 us (46%)
  waiting for transfers between devices  68.5 us (24%)
  local copies, waits for them, and re-layouts  29.7 us (10%)
  starting transfers between devices  20.6 us (7%)
  loops' own time  16.9 us (6%)
  matrix products  8.76 us (3%)
  other arithmetic  7.16 us (3%)
    all_gather x1, blocking collectives, shards(): bias_all = lax.all_gather(bias_rows, ('row', 'col'), axis=1, tiled=True)  66.4 us
    all_gather x1, blocking collectives, shards(): bias_cols = lax.all_gather(bias_next, ('row', 'col'), axis=1, tiled=True)  65.4 us
    all_to_all x4, waiting for transfers between devices, one_round(): lax.all_to_all(outgoing, ('row', 'col'), split_axis=0, concat_axis=0, til...  61.2 us
    another operation x2, loops' own time, attend_lines(): lax.map(one_block, jnp.arange(line_count * per_line, dtype=jnp.int32))  16.5 us
    all_to_all x4, starting transfers between devices, one_round(): lax.all_to_all(outgoing, ('row', 'col'), split_axis=0, concat_axis=0, til...  12.9 us
    while x24, local copies, waits for them, and re-layouts  11.2 us
    all_to_all x1, starting transfers between devices, shards(): lax.all_to_all(first_pair, ('row', 'col'), split_axis=1, concat_axis=0, t...  7.68 us
    all_to_all x1, waiting for transfers between devices, shards(): lax.all_to_all(first_pair, ('row', 'col'), split_axis=1, concat_axis=0, t...  7.28 us
  transfers between devices with their start and end apart: 5, of which 5 were waited for; matrix products, arithmetic and copies ran while one was open for 0% of the time, Pallas kernels for 0%

commit v1 on v0

--- a/solution.py
+++ b/solution.py
@@ -165,7 +165,12 @@
         normed_first.reshape(-1, channels), col_bias_proj, preferred_element_type=jnp.float32
     )
     bias_next = bias_next.reshape(rows_here, length, head_count).transpose(2, 0, 1)
-    bias_cols = lax.all_gather(bias_next, ("row", "col"), axis=1, tiled=True)
+    bias_cols = jnp.concatenate(
+        lax.all_to_all(
+            jnp.stack([bias_next] * lax.axis_size(("row", "col"))), ("row", "col"), 0, 0
+        ),
+        axis=1,
+    )
     columns = lax.all_to_all(first_pair, ("row", "col"), split_axis=1, concat_axis=0, tiled=True)
     normed_cols = layer_norm(columns).astype(jnp.bfloat16)
     projected_cols = jnp.dot(

time: 286 us -> 233 us (0.81)
  blocking collectives: 132 us -> 66.4 us
  waiting for transfers between devices: 68.5 us -> 76.2 us
  starting transfers between devices: 20.6 us -> 23.7 us
    all_gather x1 -> x0, blocking collectives: 65.4 us -> none  [shards(): bias_cols = lax.all_gather(bias_next, ('row', 'col'), axis=1, tiled=True)]
    all_to_all x0 -> x1, waiting for transfers between devices: none -> 7.76 us  [shards(): lax.all_to_all(jnp.stack([bias_next] * lax.axis_size(('row', 'col'))), ('...]
    all_to_all x0 -> x1, starting transfers between devices: none -> 4.1 us  [shards(): lax.all_to_all(jnp.stack([bias_next] * lax.axis_size(('row', 'col'))), ('...]
  transfers between devices with their start and end apart: 5 -> 6, of which waited for: 5 -> 6; matrix products, arithmetic and copies ran while one was open for 0% -> 1% of each run, Pallas kernels for 0% -> 0%
where the time goes in v1:
time: 233 us; the launch traced here: 232 us
  waiting for transfers between devices  76.2 us (33%)
  blocking collectives  66.4 us (28%)
  local copies, waits for them, and re-layouts  31.4 us (13%)
  starting transfers between devices  23.7 us (10%)
  loops' own time  16.9 us (7%)
  matrix products  8.76 us (4%)
  other arithmetic  7.16 us (3%)
    all_gather x1, blocking collectives, shards(): bias_all = lax.all_gather(bias_rows, ('row', 'col'), axis=1, tiled=True)  66.4 us
    all_to_all x4, waiting for transfers between devices, one_round(): lax.all_to_all(outgoing, ('row', 'col'), split_axis=0, concat_axis=0, til...  61 us
    another operation x2, loops' own time, attend_lines(): lax.map(one_block, jnp.arange(line_count * per_line, dtype=jnp.int32))  16.5 us
    all_to_all x4, starting transfers between devices, one_round(): lax.all_to_all(outgoing, ('row', 'col'), split_axis=0, concat_axis=0, til...  12 us
    while x24, local copies, waits for them, and re-layouts  11.2 us
    all_to_all x1, waiting for transfers between devices, shards(): lax.all_to_all(jnp.stack([bias_next] * lax.axis_size(('row', 'col'))), ('...  7.76 us
    all_to_all x1, starting transfers between devices, shards(): lax.all_to_all(first_pair, ('row', 'col'), split_axis=1, concat_axis=0, t...  7.6 us
    all_to_all x1, waiting for transfers between devices, shards(): lax.all_to_all(first_pair, ('row', 'col'), split_axis=1, concat_axis=0, t...  7.38 us
  transfers between devices with their start and end apart: 6, of which 6 were waited for; matrix products, arithmetic and copies ran while one was open for 1% of the time, Pallas kernels for 0%

profile of v1, /device:TPU:1, one launch (start us, length us, event | category | flops | bytes accessed | tf_op | source)
XLA Modules:
  0.0 231.7 jit_solution(1387202768305841097)
XLA Ops:
  0.0 1.1 copy.147
  1.6 0.9 copy-done.1
  4.7 66.4 %all_gather.3 = f32[4,128,128]{2,0,1:T(4,128)S(1)} all-gather(f32[4,4,128]{2,0,1:T(4,128)S(1)} %convolution_bitcast_fusion.2), channel_id=1, replica_groups=mesh['row'=8,'col'=4] {'row','col'}, dimensions={1}, use_global_device_ids=true | all-gather | bytes 270336 | tf_op jit(solution)/shard_map/all_gather | solution.py:137
  72.5 14.2 %while.42 = (s32[]{:T(128)}, bf16[4,128,128]{1,2,0:T(8,128)(2,1)S(1)}, s32[4]{0:T(128)S(1)}, bf16[4,128,4,32]{1,3,2,0:T(8,128)(2,1)S(1)}, pred[4,128]{1,0:T(4,12...) while((s32[]{:T(128)}, ...), condition=%wide.region_5.6_spmd, body=%wide.region_2.5_spmd.sunk | while | flops 9159427 | bytes 2038731 | solution.py:91
  88.6 7.6 %all-to-all-start.1 = ((bf16[4,128,128]{2,0,1:T(4,128)(2,1)}), bf16[4,128,128]{2,0,1:T(4,128)(2,1)S(1)}, u32[]{:S(2)}, u32[]{:S(2)}) async-start(bf16[4,128,128]{2,0,1:T(4,128)(2,1)} %copy.155), calls=%async_computation.1 | async-start | bytes 262144 | tf_op jit(solution)/shard_map/all_to_all | solution.py:174
  96.4 7.4 %all-to-all-done.1 = bf16[4,128,128]{2,0,1:T(4,128)(2,1)S(1)} async-done(((bf16[4,128,128]{2,0,1:T(4,128)(2,1)}), bf16[4,128,128]{2,0,1:T(4,128)(2,1)S(1)}, u32[]{:S(2)}, u32[]{:S(2)}) %all-to-all-start.1) | async-done | bytes 131104 | tf_op jit(solution)/shard_map/all_to_all | solution.py:174
  105.1 4.1 %all-to-all-start.2 = ((f32[32,4,4,128]{3,2,1,0:T(4,128)}), f32[32,4,4,128]{3,2,1,0:T(4,128)}, u32[]{:S(2)}, u32[]{:S(2)}) async-start(f32[32,4,4,128]{3,2,1,0:T(4,128)} %stack.2), calls=%async_computation.2 | async-start | bytes 524288 | tf_op jit(solution)/shard_map/all_to_all | solution.py:169
  112.0 7.8 %all-to-all-done.2 = f32[32,4,4,128]{3,2,1,0:T(4,128)} async-done(((f32[32,4,4,128]{3,2,1,0:T(4,128)}), f32[32,4,4,128]{3,2,1,0:T(4,128)}, u32[]{:S(2)}, u32[]{:S(2)}) %all-to-all-start.2) | async-done | bytes 262176 | tf_op jit(solution)/shard_map/all_to_all | solution.py:169
  119.8 1.0 copy.166
  120.8 13.4 %while.43 = (s32[]{:T(128)}, bf16[4,128,128]{1,2,0:T(8,128)(2,1)S(1)}, s32[4]{0:T(128)S(1)}, bf16[128,4,4,32]{0,3,2,1:T(8,128)(2,1)S(1)}, pred[4,128]{1,0:T(4,12...) while((s32[]{:T(128)}, ...), condition=%wide.region_13.14_spmd, body=%wide.region_10.13_spmd.sunk | while | flops 9159427 | bytes 2038731 | solution.py:91
  136.6 91.2 %while.44 = (s32[]{:T(128)}, f32[16,32,128]{1,0,2:T(8,128)S(1)}, bf16[8,4,16,128]{3,2,0,1:T(8,128)(2,1)S(1)}, bf16[128,4,128]{2,0,1:T(8,128)(2,1)S(1)}, bf16[128...) while((s32[]{:T(128)}, f32[16,32,128]{1,0,2:T(8,128)S(1)}, ...), condition=%wide.region_17.18_spmd.clone, body=%wide.region_16.17_spmd.clone.sunk | while | flops 5898243 | bytes 7373015 | solution.py:241
  138.2 2.5 %all-to-all-start = ((bf16[32,64,128]{2,1,0:T(8,128)(2,1)}), bf16[32,64,128]{2,1,0:T(8,128)(2,1)S(1)}, u32[]{:S(2)}, u32[]{:S(2)}) async-start(bf16[32,64,128]{2,1,0:T(8,128)(2,1)} %bitcast.190), calls=%async_computation | async-start | bytes 1048576 | tf_op jit(solution)/shard_map/while/body/eval_jaxpr/all_to_all | solution.py:225
  140.8 15.3 %all-to-all-done = bf16[32,64,128]{2,1,0:T(8,128)(2,1)S(1)} async-done(((bf16[32,64,128]{2,1,0:T(8,128)(2,1)}), bf16[32,64,128]{2,1,0:T(8,128)(2,1)S(1)}, u32[]{:S(2)}, u32[]{:S(2)}) %all-to-all-start) | async-done | bytes 524320 | tf_op jit(solution)/shard_map/while/body/eval_jaxpr/all_to_all | solution.py:225
  156.6 1.4 copy.218
  160.5 3.1 %all-to-all-start = ((bf16[32,64,128]{2,1,0:T(8,128)(2,1)}), bf16[32,64,128]{2,1,0:T(8,128)(2,1)S(1)}, u32[]{:S(2)}, u32[]{:S(2)}) async-start(bf16[32,64,128]{2,1,0:T(8,128)(2,1)} %bitcast.190), calls=%async_computation | async-start | bytes 1048576 | tf_op jit(solution)/shard_map/while/body/eval_jaxpr/all_to_all | solution.py:225
  163.7 15.3 %all-to-all-done = bf16[32,64,128]{2,1,0:T(8,128)(2,1)S(1)} async-done(((bf16[32,64,128]{2,1,0:T(8,128)(2,1)}), bf16[32,64,128]{2,1,0:T(8,128)(2,1)S(1)}, u32[]{:S(2)}, u32[]{:S(2)}) %all-to-all-start) | async-done | bytes 524320 | tf_op jit(solution)/shard_map/while/body/eval_jaxpr/all_to_all | solution.py:225
  179.5 1.4 copy.218
  183.5 3.2 %all-to-all-start = ((bf16[32,64,128]{2,1,0:T(8,128)(2,1)}), bf16[32,64,128]{2,1,0:T(8,128)(2,1)S(1)}, u32[]{:S(2)}, u32[]{:S(2)}) async-start(bf16[32,64,128]{2,1,0:T(8,128)(2,1)} %bitcast.190), calls=%async_computation | async-start | bytes 1048576 | tf_op jit(solution)/shard_map/while/body/eval_jaxpr/all_to_all | solution.py:225
  186.6 15.3 %all-to-all-done = bf16[32,64,128]{2,1,0:T(8,128)(2,1)S(1)} async-done(((bf16[32,64,128]{2,1,0:T(8,128)(2,1)}), bf16[32,64,128]{2,1,0:T(8,128)(2,1)S(1)}, u32[]{:S(2)}, u32[]{:S(2)}) %all-to-all-start) | async-done | bytes 524320 | tf_op jit(solution)/shard_map/while/body/eval_jaxpr/all_to_all | solution.py:225
  202.4 1.4 copy.218
  206.4 3.2 %all-to-all-start = ((bf16[32,64,128]{2,1,0:T(8,128)(2,1)}), bf16[32,64,128]{2,1,0:T(8,128)(2,1)S(1)}, u32[]{:S(2)}, u32[]{:S(2)}) async-start(bf16[32,64,128]{2,1,0:T(8,128)(2,1)} %bitcast.190), calls=%async_computation | async-start | bytes 1048576 | tf_op jit(solution)/shard_map/while/body/eval_jaxpr/all_to_all | solution.py:225
  209.6 15.3 %all-to-all-done = bf16[32,64,128]{2,1,0:T(8,128)(2,1)S(1)} async-done(((bf16[32,64,128]{2,1,0:T(8,128)(2,1)}), bf16[32,64,128]{2,1,0:T(8,128)(2,1)S(1)}, u32[]{:S(2)}, u32[]{:S(2)}) %all-to-all-start) | async-done | bytes 524320 | tf_op jit(solution)/shard_map/while/body/eval_jaxpr/all_to_all | solution.py:225
  225.4 1.4 copy.218
  230.7 1.0 fusion.41
  (233 shorter events, 37.6 us)
Async XLA Ops:
  0.0 1.2 copy-start
  1.5 1.0 copy-start.1
  3.2 0.7 copy-start.11
  3.9 0.7 copy-start.13
  71.5 1.0 slice-start
  71.6 0.8 copy-start.4
  72.5 14.2 %copy-start.10 = (bf16[128,128]{1,0:T(8,128)(2,1)S(1)}, bf16[128,128]{1,0:T(8,128)(2,1)}, u32[]{:S(2)}) copy-start(bf16[128,128]{1,0:T(8,128)(2,1)} %param.26) | copy-start | bytes 98308
  87.8 0.7 copy-start.14
  88.6 15.1 %all-to-all-start.1 = ((bf16[4,128,128]{2,0,1:T(4,128)(2,1)}), bf16[4,128,128]{2,0,1:T(4,128)(2,1)S(1)}, u32[]{:S(2)}, u32[]{:S(2)}) async-start(bf16[4,128,128]{2,0,1:T(4,128)(2,1)} %copy.155), calls=%async_computation.1 | async-start | bytes 262144 | tf_op jit(solution)/shard_map/all_to_all | solution.py:174
  105.1 14.6 %all-to-all-start.2 = ((f32[32,4,4,128]{3,2,1,0:T(4,128)}), f32[32,4,4,128]{3,2,1,0:T(4,128)}, u32[]{:S(2)}, u32[]{:S(2)}) async-start(f32[32,4,4,128]{3,2,1,0:T(4,128)} %stack.2), calls=%async_computation.2 | async-start | bytes 524288 | tf_op jit(solution)/shard_map/all_to_all | solution.py:169
  110.4 0.9 copy-start.5
  120.8 13.4 %copy-start.8 = (bf16[128,128]{1,0:T(8,128)(2,1)S(1)}, bf16[128,128]{1,0:T(8,128)(2,1)}, u32[]{:S(2)}) copy-start(bf16[128,128]{1,0:T(8,128)(2,1)} %param.29) | copy-start | bytes 98308
  134.5 0.8 copy-start.6
  135.3 0.8 copy-start.7
  138.2 17.8 %all-to-all-start = ((bf16[32,64,128]{2,1,0:T(8,128)(2,1)}), bf16[32,64,128]{2,1,0:T(8,128)(2,1)S(1)}, u32[]{:S(2)}, u32[]{:S(2)}) async-start(bf16[32,64,128]{2,1,0:T(8,128)(2,1)} %bitcast.190), calls=%async_computation | async-start | bytes 1048576 | tf_op jit(solution)/shard_map/while/body/eval_jaxpr/all_to_all | solution.py:225
  158.0 0.9 copy-start.3
  160.5 18.4 %all-to-all-start = ((bf16[32,64,128]{2,1,0:T(8,128)(2,1)}), bf16[32,64,128]{2,1,0:T(8,128)(2,1)S(1)}, u32[]{:S(2)}, u32[]{:S(2)}) async-start(bf16[32,64,128]{2,1,0:T(8,128)(2,1)} %bitcast.190), calls=%async_computation | async-start | bytes 1048576 | tf_op jit(solution)/shard_map/while/body/eval_jaxpr/all_to_all | solution.py:225
  181.0 0.9 copy-start.3
  183.5 18.4 %all-to-all-start = ((bf16[32,64,128]{2,1,0:T(8,128)(2,1)}), bf16[32,64,128]{2,1,0:T(8,128)(2,1)S(1)}, u32[]{:S(2)}, u32[]{:S(2)}) async-start(bf16[32,64,128]{2,1,0:T(8,128)(2,1)} %bitcast.190), calls=%async_computation | async-start | bytes 1048576 | tf_op jit(solution)/shard_map/while/body/eval_jaxpr/all_to_all | solution.py:225
  203.9 0.9 copy-start.3
  206.4 18.4 %all-to-all-start = ((bf16[32,64,128]{2,1,0:T(8,128)(2,1)}), bf16[32,64,128]{2,1,0:T(8,128)(2,1)S(1)}, u32[]{:S(2)}, u32[]{:S(2)}) async-start(bf16[32,64,128]{2,1,0:T(8,128)(2,1)} %bitcast.190), calls=%async_computation | async-start | bytes 1048576 | tf_op jit(solution)/shard_map/while/body/eval_jaxpr/all_to_all | solution.py:225
  226.8 0.9 copy-start.3
  229.2 0.8 copy-start.12
  229.9 0.8 copy-start.9
  (4 other events, 2.6 us)
